TPU v7x, 512 devices: a whole 4x4x16 slice. The times are simulated.
512 devices in a mesh: blk: 64 (over y_lo, z, core), exp: 8 (over y_hi, x).
Axes of the slice: x: 4, y: 4 (y_hi: 2, y_lo: 2; y = y_hi * 2 + y_lo), z: 16, core: 2. Of those that a mesh axis runs over, the one named last changes fastest.
Arguments:
- hidden_in: bfloat16 [32, 4, 2048], P('exp'), may hold values from -3 to 3
- q_lat: bfloat16 [32, 4, 16, 512], P('exp'), may hold values from -28 to 28
- q_rope: bfloat16 [32, 4, 16, 64], P('exp'), may hold values from -4 to 4
- new_lat: bfloat16 [32, 4, 512], P('exp'), may hold values from -4 to 4
- new_rope: bfloat16 [32, 4, 64], P('exp'), may hold values from -4 to 4
- cache_lat: bfloat16 [32, 16384, 512], P('exp', 'blk'), may hold values from -4 to 4
- cache_rope: bfloat16 [32, 16384, 64], P('exp', 'blk'), may hold values from -4 to 4
- lengths: int32 [32], P('exp'), may hold values from 2 to 16384, as said below
- w_uv: bfloat16 [512, 2048], P(None, 'blk'), may hold values from -3 to 3
- w_out: bfloat16 [2048, 2048], P('blk'), may hold values from -0.125 to 0.125
- norm_gain: float32 [2048], replicated, may hold values from 0.1 to 1.9
- w_router: bfloat16 [2048, 64], replicated, may hold values from -0.125 to 0.125
- routes: int32 [32, 4, 6], P('exp'), may hold values from 0 to 63, all different within a row; in each aligned block of 16 rows (0 to 15, 16 to 31, ..., all dimensions but the last counted through in order) at most 3 rows name the same one
- w_gate: bfloat16 [64, 2048, 1408], P('blk', None, 'exp'), may hold values from -0.125 to 0.125
- w_up: bfloat16 [64, 2048, 1408], P('blk', None, 'exp'), may hold values from -0.125 to 0.125
- w_down: bfloat16 [64, 1408, 2048], P('blk', 'exp'), may hold values from -0.15625 to 0.15625
Outputs:
- hidden_out: bfloat16 [32, 4, 2048], P('exp')
Inputs may be any that keep to these rules, and one draw needn't show every extreme that they name: `lengths`: in each aligned group of 4 requests exactly 1 have length 16384; the others have 2 to 512. `routes`: each row names 6 different experts; in the 16 rows of one index of exp no expert is named more than 3 times.
All inputs are finite; a program needn't handle non-finite values.
Results may differ from a plain program's by a relative error of at most 0.0062.
Values may be sent and summed in bfloat16 or wider, within the bound.
No kernel may reach another device: no remote copies, remote signals or barrier semaphores. Data moves between devices by JAX's collectives and lax.ppermute only.
A program may use at most 128 MiB of HBM per device.

v0:
```python
import jax
import jax.numpy as jnp
from jax import lax
from jax.sharding import PartitionSpec as P

V = 128
QK = 192
CAP = 3
NEG_FILL = -1e30
ROUTE_SCALE = 2.446
NORM_EPS = 1e-06


def merged_2(x, axis, combine):
    everything = jax.tree.map(lambda part: lax.all_gather(part, axis), x)
    leading = jax.tree.map(lambda part: part[0], everything)

    def step(k, so_far):
        return combine(so_far, jax.tree.map(lambda part: part[k], everything))

    return lax.fori_loop(1, lax.axis_size(axis), step, leading)


def block_partial(query, query_rope, keys_lat, keys_rope, valid):
    scale = QK ** (-0.5)
    scores = (
        jnp.einsum("rmc,rkc->rmk", query, keys_lat, preferred_element_type=jnp.float32)
        + jnp.einsum("rmc,rkc->rmk", query_rope, keys_rope, preferred_element_type=jnp.float32)
    ) * scale
    masked = jnp.where(valid, scores, NEG_FILL)
    peak_val = jnp.max(masked, axis=2)
    weights = jnp.where(valid, jnp.exp(masked - peak_val[:, :, None]), 0.0)
    weight_sum = jnp.sum(weights, axis=2)
    summed = jnp.einsum(
        "rmk,rkc->rmc", weights.astype(jnp.bfloat16), keys_lat, preferred_element_type=jnp.float32
    )
    return (peak_val, weight_sum, summed)


def merge_pair(left_part, right_part):
    peak_left, total_left, sum_left = left_part
    peak_right, total_right, sum_right = right_part
    peak_val = jnp.maximum(peak_left, peak_right)
    factor_left = jnp.exp(peak_left - peak_val)
    factor_right = jnp.exp(peak_right - peak_val)
    weight_sum = factor_left * total_left + factor_right * total_right
    summed = factor_left[..., None] * sum_left + factor_right[..., None] * sum_right
    return (peak_val, weight_sum, summed)


def local(
    hidden_in,
    q_lat,
    q_rope,
    new_lat,
    new_rope,
    cache_lat,
    cache_rope,
    lengths,
    w_uv,
    w_out,
    norm_gain,
    w_router,
    routes,
    w_gate,
    w_up,
    w_down,
):
    requests, new_steps, head_count, latent_dim = q_lat.shape
    query_rows = new_steps * head_count
    query = q_lat.reshape(requests, query_rows, latent_dim)
    query_rope = q_rope.reshape(requests, query_rows, q_rope.shape[3])
    cache_span = cache_lat.shape[1]
    position = lax.axis_index("blk") * cache_span + lax.iota(jnp.int32, cache_span)
    cache_valid = jnp.broadcast_to(
        position[None, None, :] < lengths[:, None, None], (requests, query_rows, cache_span)
    )
    cache_part = block_partial(query, query_rope, cache_lat, cache_rope, cache_valid)
    token_of_row = lax.iota(jnp.int32, query_rows) // head_count
    fresh_valid = lax.iota(jnp.int32, new_steps)[None, :] <= token_of_row[:, None]
    fresh_valid = jnp.broadcast_to(fresh_valid[None, :, :], (requests, query_rows, new_steps))
    fresh_part = block_partial(query, query_rope, new_lat, new_rope, fresh_valid)
    merged = merged_2(cache_part, "blk", merge_pair)
    peak_val, weight_sum, summed = merge_pair(merged, fresh_part)
    lat_out = (summed / weight_sum[:, :, None]).astype(jnp.bfloat16)
    token_rows = requests * new_steps
    head_cols = w_uv.shape[1]
    head_pick = lax.axis_index("blk") * head_cols // V
    lat_heads = lat_out.reshape(requests, new_steps, head_count, latent_dim)
    lat_head = lax.dynamic_index_in_dim(lat_heads, head_pick, axis=2, keepdims=False).reshape(
        token_rows, latent_dim
    )
    heads_out = jnp.dot(lat_head, w_uv, preferred_element_type=jnp.float32).astype(jnp.bfloat16)
    proj_part = jnp.dot(heads_out, w_out, preferred_element_type=jnp.float32)
    projected = lax.psum(proj_part, "blk")
    width = hidden_in.shape[2]
    mixed = hidden_in.reshape(token_rows, width).astype(jnp.float32) + projected
    meansq = jnp.mean(mixed * mixed, axis=1, keepdims=True)
    normed = (mixed * lax.rsqrt(meansq + NORM_EPS) * norm_gain[None, :]).astype(jnp.bfloat16)
    affinity = jax.nn.sigmoid(jnp.dot(normed, w_router, preferred_element_type=jnp.float32))
    expert_total = w_router.shape[1]
    top_count = routes.shape[2]
    flat_routes = routes.reshape(token_rows, top_count)
    route_hits = flat_routes[:, :, None] == lax.iota(jnp.int32, expert_total)[None, None, :]
    chosen = jnp.sum(jnp.where(route_hits, affinity[:, None, :], 0.0), axis=2)
    route_weight = ROUTE_SCALE * chosen / jnp.sum(chosen, axis=1, keepdims=True)
    local_count = w_gate.shape[0]
    local_ids = lax.axis_index("blk") * local_count + lax.iota(jnp.int32, local_count)
    pair_routes = flat_routes.reshape(token_rows * top_count)
    local_hits = (pair_routes[:, None] == local_ids[None, :]).astype(jnp.int32)
    ranks = jnp.cumsum(local_hits, axis=0) - 1
    slot_ids = lax.iota(jnp.int32, CAP)
    slot_match = local_hits.T[:, None, :] * (ranks.T[:, None, :] == slot_ids[None, :, None]).astype(
        jnp.int32
    )
    select = slot_match.reshape(local_count, CAP, token_rows, top_count).astype(jnp.float32)
    dispatch_map = jnp.sum(select, axis=3)
    combine_map = jnp.sum(select * route_weight[None, None, :, :], axis=3)
    dispatched = jnp.einsum(
        "esr,rd->esd", dispatch_map.astype(jnp.bfloat16), normed, preferred_element_type=jnp.float32
    ).astype(jnp.bfloat16)
    piece = lax.all_gather(dispatched, "exp", axis=1, tiled=True)
    gate = jnp.einsum("erd,edf->erf", piece, w_gate, preferred_element_type=jnp.float32)
    upper = jnp.einsum("erd,edf->erf", piece, w_up, preferred_element_type=jnp.float32)
    hidden_all = (jax.nn.silu(gate) * upper).astype(jnp.bfloat16)
    partial_out = jnp.einsum("erf,efd->erd", hidden_all, w_down, preferred_element_type=jnp.float32)
    expert_out = lax.psum_scatter(partial_out, "exp", scatter_dimension=1, tiled=True)
    moe_part = jnp.einsum("esr,esd->rd", combine_map, expert_out, precision=lax.Precision.HIGHEST)
    moe_all = lax.psum(moe_part, "blk")
    result = (mixed + moe_all).astype(jnp.bfloat16)
    return result.reshape(requests, new_steps, width)


def solution(mesh):
    in_specs = (
        P("exp", None, None),
        P("exp", None, None, None),
        P("exp", None, None, None),
        P("exp", None, None),
        P("exp", None, None),
        P("exp", "blk", None),
        P("exp", "blk", None),
        P("exp"),
        P(None, "blk"),
        P("blk", None),
        P(),
        P(),
        P("exp", None, None),
        P("blk", None, "exp"),
        P("blk", None, "exp"),
        P("blk", "exp", None),
    )
    out_specs = P("exp", None, None)
    return jax.shard_map(local, mesh=mesh, in_specs=in_specs, out_specs=out_specs, check_vma=False)
```

profile of v0, /device:TPU:24, one launch (start us, length us, event | category | flops | bytes accessed | tf_op | source)
XLA Modules:
  0.0 1199.8 jit_solution(7835807839142678732)
XLA Ops:
  7.8 1.4 fusion.56
  11.8 70.6 %all-gather.5 = f32[64,4,64]{2,1,0:T(4,128)S(1)} all-gather(f32[1,4,64]{2,1,0:T(4,128)S(1)} %bitcast.74), channel_id=3, replica_groups=mesh['blk'=64,'exp'=8] {'blk'}, dimensions={0}, use_global_device_ids=true | all-gather | bytes 66560 | tf_op jit(solution)/shard_map/all_gather | solution.py:15
  82.4 61.4 %all-gather.4 = f32[64,4,64]{2,1,0:T(4,128)S(1)} all-gather(f32[1,4,64]{2,1,0:T(4,128)S(1)} %bitcast.73), channel_id=2, replica_groups=mesh['blk'=64,'exp'=8] {'blk'}, dimensions={0}, use_global_device_ids=true | all-gather | bytes 66560 | tf_op jit(solution)/shard_map/all_gather | solution.py:15
  146.7 65.1 %all-gather.9.cloned.1.call-done = f32[256,64,512]{2,1,0:T(8,128)} async-done(((f32[4,64,512]{2,1,0:T(8,128)}), f32[256,64,512]{2,1,0:T(8,128)}) %all-gather.9.cloned.1.call-update) | async-done | bytes 33554448 | tf_op jit(solution)/shard_map/all_gather | solution.py:15
  212.9 79.7 %while.19 = (s32[]{:T(128)}, f32[4,64]{1,0:T(4,128)S(1)}, f32[4,64]{1,0:T(4,128)S(1)}, f32[4,64,512]{2,1,0:T(8,128)S(1)}, f32[64,4,64]{2,1,0:T(4,128)S(1)}, /*in...) while((s32[]{:T(128)}, f32[4,64]{1,0:T(4,128)S(1)}, ...), condition=%wide.region_3.4_spmd, body=%wide.region_2.3_spmd.sunk | while | flops 394757 | bytes 1583255 | solution.py:21
  212.9 1.2 fusion.79
  214.2 1.2 fusion.79
  215.5 1.2 fusion.79
  220.5 1.2 fusion.79
  221.8 1.2 fusion.79
  223.1 1.2 fusion.79
  224.3 1.2 fusion.79
  228.1 1.2 fusion.79
  229.4 1.2 fusion.79
  230.7 1.2 fusion.79
  231.9 1.2 fusion.79
  235.7 1.2 fusion.79
  237.0 1.2 fusion.79
  238.2 1.2 fusion.79
  239.5 1.2 fusion.79
  244.6 1.2 fusion.79
  245.8 1.2 fusion.79
  247.1 1.2 fusion.79
  248.4 1.2 fusion.79
  252.2 1.2 fusion.79
  253.4 1.2 fusion.79
  254.7 1.2 fusion.79
  256.0 1.2 fusion.79
  259.8 1.2 fusion.79
  261.0 1.2 fusion.79
  262.3 1.2 fusion.79
  263.5 1.2 fusion.79
  268.6 1.2 fusion.79
  269.9 1.2 fusion.79
  271.1 1.2 fusion.79
  272.4 1.2 fusion.79
  276.2 1.2 fusion.79
  277.5 1.2 fusion.79
  278.7 1.2 fusion.79
  280.0 1.2 fusion.79
  293.8 1.9 fusion.15
  298.7 375.5 %all-reduce.5.cloned.1.call-done = f32[16,2048]{1,0:T(8,128)} async-done(((f32[16,2048]{1,0:T(8,128)}), f32[16,2048]{1,0:T(8,128)}) %all-reduce.5.cloned.1.call-update) | async-done | bytes 131088 | tf_op jit(solution)/shard_map/psum | solution.py:95
  677.6 34.2 %all-gather.6 = bf16[8,3,2048]{2,1,0:T(4,128)(2,1)S(1)} all-gather(bf16[1,3,2048]{2,1,0:T(4,128)(2,1)S(1)} %fusion.3), channel_id=5, replica_groups=mesh['blk'=64,'exp'=8] {'exp'}, dimensions={0}, use_global_device_ids=true | all-gather | bytes 110592 | tf_op jit(solution)/shard_map/all_gather | solution.py:122
  711.9 1.4 fusion.19
  713.3 2.0 convolution_bitcast_fusion
  716.3 1.3 dynamic-slice
  718.2 93.9 %all-reduce.9.cloned.1.call-done = f32[1,24,2048]{2,0,1:T(1,128)} async-done(((f32[1,24,2048]{2,0,1:T(1,128)}), f32[1,24,2048]{2,0,1:T(1,128)}) %all-reduce.9.cloned.1.call-update) | async-done | bytes 196624
  813.9 377.7 %all-reduce.7.cloned.1.call-done = f32[16,2048]{1,0:T(8,128)} async-done(((f32[16,2048]{1,0:T(8,128)}), f32[16,2048]{1,0:T(8,128)}) %all-reduce.7.cloned.1.call-update) | async-done | bytes 131088 | tf_op jit(solution)/shard_map/psum | solution.py:129
  (141 shorter events, 55.3 us)
Async XLA Ops:
  6.5 1.2 copy-start
  6.5 205.3 %all-gather.9.cloned.1.call-start = ((), (), s32[]{:S(2)}) async-start(), calls=%async_computation.2 | async-start | bytes 34078720 | tf_op jit(solution)/shard_map/all_gather | solution.py:15
  11.5 662.7 %all-reduce.5.cloned.1.call-start = ((), (), s32[]{:S(2)}) async-start(), calls=%async_computation | async-start | bytes 262144 | tf_op jit(solution)/shard_map/psum | solution.py:95
  295.7 516.5 %all-reduce.9.cloned.1.call-start = ((), (), s32[]{:S(2)}) async-start(), calls=%async_computation.3 | async-start | bytes 393216
  716.3 475.4 %all-reduce.7.cloned.1.call-start = ((), (), s32[]{:S(2)}) async-start(), calls=%async_computation.1 | async-start | bytes 262144 | tf_op jit(solution)/shard_map/psum | solution.py:129
Sparse Core Ops, SparseCore 0:
  11.6 200.1 all-gather.8
  295.8 378.3 all-reduce.4
  716.4 95.6 all-reduce.8
  814.9 376.7 all-reduce.6
where the time goes:
time: 1200 us
  waiting for transfers between devices  912 us (76%)
  blocking collectives  166 us (14%)
  other arithmetic  82.9 us (7%)
  matrix products  15.3 us (1%)
  between operations  13.9 us (1%)
    psum x1, waiting for transfers between devices, local(): moe_all = lax.psum(moe_part, 'blk')  378 us
    psum x1, waiting for transfers between devices, local(): projected = lax.psum(proj_part, 'blk')  376 us
    all_gather x2, blocking collectives, merged_2(): everything = jax.tree.map(lambda part: lax.all_gather(part, axis), x)  132 us
    unnamed x5, waiting for transfers between devices  94 us
    add x63, other arithmetic, merge_pair(): factor_left[..., None] * sum_left + factor_right[..., None] * sum_right  76.3 us
    all_gather x1, waiting for transfers between devices, merged_2(): everything = jax.tree.map(lambda part: lax.all_gather(part, axis), x)  65.1 us
    all_gather x1, blocking collectives, local(): piece = lax.all_gather(dispatched, 'exp', axis=1, tiled=True)  34.2 us
  transfers between devices with their start and end apart: 4, of which 4 were waited for; matrix products, arithmetic and copies ran while one was open for 1% of the time, Pallas kernels for 0%

commit v1 on v0

--- a/solution.py
+++ b/solution.py
@@ -92,7 +92,7 @@
     )
     heads_out = jnp.dot(lat_head, w_uv, preferred_element_type=jnp.float32).astype(jnp.bfloat16)
     proj_part = jnp.dot(heads_out, w_out, preferred_element_type=jnp.float32)
-    projected = lax.psum(proj_part, "blk")
+    projected = jnp.sum(lax.all_gather(proj_part, "blk"), axis=0)
     width = hidden_in.shape[2]
     mixed = hidden_in.reshape(token_rows, width).astype(jnp.float32) + projected
     meansq = jnp.mean(mixed * mixed, axis=1, keepdims=True)

time: 1200 us -> 958 us (0.80)
  waiting for transfers between devices: 912 us -> 662 us
    psum x1 -> x0, waiting for transfers between devices: 376 us -> none  [local(): projected = lax.psum(proj_part, 'blk')]
    all_gather x0 -> x1, waiting for transfers between devices: none -> 125 us  [local(): projected = jnp.sum(lax.all_gather(proj_part, 'blk'), axis=0)]
where the time goes in v1:
time: 958 us; the launch traced here: 954 us
  waiting for transfers between devices  662 us (69%)
  blocking collectives  166 us (17%)
  other arithmetic  88.5 us (9%)
  matrix products  14.5 us (2%)
  between operations  13.9 us (1%)
    psum x1, waiting for transfers between devices, local(): moe_all = lax.psum(moe_part, 'blk')  378 us
    all_gather x2, blocking collectives, merged_2(): everything = jax.tree.map(lambda part: lax.all_gather(part, axis), x)  132 us
    all_gather x1, waiting for transfers between devices, local(): projected = jnp.sum(lax.all_gather(proj_part, 'blk'), axis=0)  125 us
    unnamed x5, waiting for transfers between devices  93.1 us
    add x63, other arithmetic, merge_pair(): factor_left[..., None] * sum_left + factor_right[..., None] * sum_right  77.2 us
    all_gather x1, waiting for transfers between devices, merged_2(): everything = jax.tree.map(lambda part: lax.all_gather(part, axis), x)  65.8 us
    all_gather x1, blocking collectives, local(): piece = lax.all_gather(dispatched, 'exp', axis=1, tiled=True)  34.2 us
  transfers between devices with their start and end apart: 4, of which 4 were waited for; matrix products, arithmetic and copies ran while one was open for 1% of the time, Pallas kernels for 0%

profile of v1, /device:TPU:24, one launch (start us, length us, event | category | flops | bytes accessed | tf_op | source)
XLA Modules:
  0.0 954.0 jit_solution(2277064533416841878)
XLA Ops:
  7.8 1.4 fusion.58
  11.8 70.6 %all-gather.6 = f32[64,4,64]{2,1,0:T(4,128)S(1)} all-gather(f32[1,4,64]{2,1,0:T(4,128)S(1)} %bitcast.77), channel_id=3, replica_groups=mesh['blk'=64,'exp'=8] {'blk'}, dimensions={0}, use_global_device_ids=true | all-gather | bytes 66560 | tf_op jit(solution)/shard_map/all_gather | solution.py:15
  82.4 61.4 %all-gather.5 = f32[64,4,64]{2,1,0:T(4,128)S(1)} all-gather(f32[1,4,64]{2,1,0:T(4,128)S(1)} %bitcast.76), channel_id=2, replica_groups=mesh['blk'=64,'exp'=8] {'blk'}, dimensions={0}, use_global_device_ids=true | all-gather | bytes 66560 | tf_op jit(solution)/shard_map/all_gather | solution.py:15
  146.0 65.8 %all-gather.11.cloned.1.call-done = f32[256,64,512]{2,1,0:T(8,128)} async-done(((f32[4,64,512]{2,1,0:T(8,128)}), f32[256,64,512]{2,1,0:T(8,128)}) %all-gather.11.cloned.1.call-update) | async-done | bytes 33554448 | tf_op jit(solution)/shard_map/all_gather | solution.py:15
  212.9 80.6 %while.19 = (s32[]{:T(128)}, f32[4,64]{1,0:T(4,128)S(1)}, f32[4,64]{1,0:T(4,128)S(1)}, f32[4,64,512]{2,1,0:T(8,128)S(1)}, f32[64,4,64]{2,1,0:T(4,128)S(1)}, /*in...) while((s32[]{:T(128)}, f32[4,64]{1,0:T(4,128)S(1)}, ...), condition=%wide.region_3.4_spmd, body=%wide.region_2.3_spmd.sunk | while | flops 394757 | bytes 1583255 | solution.py:21
  212.9 1.2 fusion.82
  214.2 1.2 fusion.82
  215.5 1.2 fusion.82
  216.8 1.2 fusion.82
  219.3 1.2 fusion.82
  220.6 1.2 fusion.82
  223.2 1.2 fusion.82
  224.4 1.2 fusion.82
  225.7 1.2 fusion.82
  227.0 1.2 fusion.82
  228.3 1.2 fusion.82
  229.6 1.2 fusion.82
  230.8 1.2 fusion.82
  233.4 1.2 fusion.82
  234.7 1.2 fusion.82
  236.0 1.2 fusion.82
  237.2 1.2 fusion.82
  238.5 1.2 fusion.82
  239.8 1.2 fusion.82
  241.1 1.2 fusion.82
  243.6 1.2 fusion.82
  244.9 1.2 fusion.82
  247.5 1.2 fusion.82
  248.7 1.2 fusion.82
  250.0 1.2 fusion.82
  251.3 1.2 fusion.82
  252.6 1.2 fusion.82
  253.9 1.2 fusion.82
  255.1 1.2 fusion.82
  257.7 1.2 fusion.82
  259.0 1.2 fusion.82
  260.3 1.2 fusion.82
  261.5 1.2 fusion.82
  262.8 1.2 fusion.82
  294.7 1.9 fusion.15
  300.3 124.9 %all-gather.13.cloned.1.call-done = f32[1024,2048]{1,0:T(8,128)} async-done(((f32[16,2048]{1,0:T(8,128)}), f32[1024,2048]{1,0:T(8,128)}) %all-gather.13.cloned.1.call-update) | async-done | bytes 8388624 | tf_op jit(solution)/shard_map/all_gather | solution.py:95
  425.1 3.8 reduce_sum.76
  432.7 34.2 %all-gather.7 = bf16[8,3,2048]{2,1,0:T(4,128)(2,1)S(1)} all-gather(bf16[1,3,2048]{2,1,0:T(4,128)(2,1)S(1)} %fusion.3), channel_id=6, replica_groups=mesh['blk'=64,'exp'=8] {'exp'}, dimensions={0}, use_global_device_ids=true | all-gather | bytes 110592 | tf_op jit(solution)/shard_map/all_gather | solution.py:122
  466.9 1.4 fusion.19
  468.3 2.0 convolution_bitcast_fusion
  471.3 1.3 dynamic-slice
  473.3 93.1 %all-reduce.6.cloned.1.call-done = f32[1,24,2048]{2,0,1:T(1,128)} async-done(((f32[1,24,2048]{2,0,1:T(1,128)}), f32[1,24,2048]{2,0,1:T(1,128)}) %all-reduce.6.cloned.1.call-update) | async-done | bytes 196624
  568.1 377.7 %all-reduce.4.cloned.1.call-done = f32[16,2048]{1,0:T(8,128)} async-done(((f32[16,2048]{1,0:T(8,128)}), f32[16,2048]{1,0:T(8,128)}) %all-reduce.4.cloned.1.call-update) | async-done | bytes 131088 | tf_op jit(solution)/shard_map/psum | solution.py:129
  (147 shorter events, 57.2 us)
Async XLA Ops:
  6.5 1.2 copy-start
  6.5 205.3 %all-gather.11.cloned.1.call-start = ((), (), s32[]{:S(2)}) async-start(), calls=%async_computation.1 | async-start | bytes 34078720 | tf_op jit(solution)/shard_map/all_gather | solution.py:15
  11.5 413.6 %all-gather.13.cloned.1.call-start = ((), (), s32[]{:S(2)}) async-start(), calls=%async_computation.2 | async-start | bytes 8519680 | tf_op jit(solution)/shard_map/all_gather | solution.py:95
  296.5 269.8 %all-reduce.6.cloned.1.call-start = ((), (), s32[]{:S(2)}) async-start(), calls=%async_computation.3 | async-start | bytes 393216
  471.3 474.6 %all-reduce.4.cloned.1.call-start = ((), (), s32[]{:S(2)}) async-start(), calls=%async_computation | async-start | bytes 262144 | tf_op jit(solution)/shard_map/psum | solution.py:129
Sparse Core Ops, SparseCore 0:
  11.6 200.1 all-gather.10
  296.7 128.4 all-gather.12
  471.4 94.8 all-reduce.5
  569.1 376.7 all-reduce.3
